TPU v7x, 256 devices: a whole 4x4x8 slice. The times are simulated.
256 devices in a mesh: pair: 2 (over core), seq: 32 (over y, x, z_hi), tp: 4 (over z_lo).
Axes of the slice: x: 4, y: 4, z: 8 (z_hi: 2, z_lo: 4; z = z_hi * 4 + z_lo), core: 2. Of those that a mesh axis runs over, the one named last changes fastest.
Arguments:
- hidden: bfloat16 [36864, 3072], P(('pair', 'seq'), 'tp'), may hold values from -11 to 11
- positions: int32 [3, 36864], P(None, ('pair', 'seq')), may hold values from 0 to 63, as said below
- lengths: int32 [8], P('pair'), may hold values from 1 to 512, as said below
- step_index: int32 [1], replicated, may hold values from 0 to 7
- layer_mod: float32 [8, 3, 3072], P('pair'), may hold values from -3 to 3
- final_mod: float32 [8, 2, 3072], P('pair'), may hold values from -3 to 3
- qkv_weight: bfloat16 [3072, 3, 1536], P(None, None, 'tp'), may hold values from -0.108253175 to 0.108253175
- q_gain: float32 [128], replicated, may hold values from 0.5 to 5.5
- k_gain: float32 [128], replicated, may hold values from 0.5 to 5.5
- out_weight: bfloat16 [1536, 3072], P('tp'), may hold values from -0.15625 to 0.15625
- final_weight: bfloat16 [3072, 64], P('tp'), may hold values from -0.109375 to 0.109375
- latents: float32 [16384, 64], P(('pair', 'seq')), may hold values from -6 to 6
Outputs:
- new_hidden: bfloat16 [36864, 3072], P(('pair', 'seq'), 'tp')
- attention_lse: float32 [12, 36864], P('tp', ('pair', 'seq'))
- next_latents: float32 [16384, 64], P(('pair', 'seq'))
Inputs may be any that keep to these rules, and one draw needn't show every extreme that they name: `lengths`: some sequence has all 512 text tokens live and some sequence just one. `positions`: the first component is zero; text rows are zero; the image rows of a sequence hold each cell (row, column) of a grid 64 cells wide exactly once, the same for both sequences of a prompt.
All inputs are finite; a program needn't handle non-finite values.
Results may differ from a plain program's by a relative error of at most 0.01.
Values may be sent and summed in bfloat16 or wider, within the bound.
No kernel may reach another device: no remote copies, remote signals or barrier semaphores. Data moves between devices by JAX's collectives and lax.ppermute only.
A program may use at most 128 MiB of HBM per device.

v0:
```python
import jax
import jax.numpy as jnp
from jax import lax
from jax.sharding import PartitionSpec as P

ROPE_T = 16
ROPE_H = 56
ROPE_W = 56
STEPS = 8
IMG_DEV = 512
TXT_DEV = 64
GUIDE = 3.5
SHIFT = 3.0


def swapped(block, axis, bit):
    count = lax.axis_size(axis)
    route = []
    for low in range(count):
        high = low | 1 << bit
        if high != low and high < count:
            route += [(low, high), (high, low)]
    return lax.ppermute(block, axis, route)


def rope_angles(ids_block):
    angle_parts = []
    for axis_pos, rope_width in ((0, ROPE_T), (1, ROPE_H), (2, ROPE_W)):
        frequencies = 10000.0 ** (-jnp.arange(0, rope_width, 2).astype(jnp.float32) / rope_width)
        angle_parts.append(ids_block[axis_pos].astype(jnp.float32)[:, None] * frequencies[None, :])
    angles = jnp.concatenate(angle_parts, axis=1)
    return (jnp.cos(angles), jnp.sin(angles))


def rotate(tensor, cosine, sine_part):
    dims_in = tensor.shape
    pair_view = tensor.reshape(dims_in[0], dims_in[1], dims_in[2] // 2, 2)
    first_part = pair_view[..., 0]
    second_part = pair_view[..., 1]
    cosine = cosine[:, None, :]
    sine_part = sine_part[:, None, :]
    turned = jnp.stack(
        [
            cosine * first_part - sine_part * second_part,
            sine_part * first_part + cosine * second_part,
        ],
        axis=-1,
    )
    return turned.reshape(dims_in)


def rms_gain(tensor, gain_vec):
    return tensor * lax.rsqrt(jnp.mean(tensor * tensor, axis=-1, keepdims=True) + 1e-06) * gain_vec


def modulate(features, shift_vec, scale_vec):
    row_mean = jnp.mean(features, axis=-1, keepdims=True)
    row_var = jnp.mean(features * features, axis=-1, keepdims=True) - row_mean * row_mean
    return (features - row_mean) * lax.rsqrt(row_var + 1e-06) * (1.0 + scale_vec) + shift_vec


def sigma_at(step_now):
    time_now = 1.0 - step_now.astype(jnp.float32) / STEPS
    return SHIFT * time_now / (1.0 + (SHIFT - 1.0) * time_now)


def attend_block(softmax_state, queries, packet, anchor, text_count):
    rows_dev = IMG_DEV + TXT_DEV
    piece_count = packet.shape[1] // rows_dev
    offset = jnp.arange(rows_dev, dtype=jnp.int32)
    score_scale = queries.shape[-1] ** (-0.5)

    def fold_piece(piece_idx, carried):
        row_max, row_sum, weighted = carried
        key_piece = lax.dynamic_slice_in_dim(packet, piece_idx * rows_dev, rows_dev, 1)
        text_index = (anchor + piece_idx) * TXT_DEV + offset - IMG_DEV
        is_live = (offset < IMG_DEV) | (text_index < text_count)
        scores = (
            jnp.einsum("qhd,khd->hqk", queries, key_piece[0], preferred_element_type=jnp.float32)
            * score_scale
        )
        scores = jnp.where(is_live[None, None, :], scores, -jnp.inf)
        new_max = jnp.maximum(row_max, jnp.max(scores, axis=2))
        exps = jnp.exp(scores - new_max[:, :, None])
        decay = jnp.exp(row_max - new_max)
        row_sum = row_sum * decay + jnp.sum(exps, axis=2)
        weighted = weighted * decay[:, :, None] + jnp.einsum(
            "hqk,khd->hqd",
            exps.astype(jnp.bfloat16),
            key_piece[1],
            preferred_element_type=jnp.float32,
        )
        return (new_max, row_sum, weighted)

    return lax.fori_loop(0, piece_count, fold_piece, softmax_state)


def on_device(
    hidden,
    positions,
    lengths,
    step_index,
    layer_mod,
    final_mod,
    qkv_weight,
    q_gain,
    k_gain,
    out_weight,
    final_weight,
    latents,
):
    spread = lax.axis_size("seq") // 4
    bit_count = spread.bit_length() - 1
    seq_pos = lax.axis_index("seq")
    local_seq = seq_pos // spread
    shard_pos = seq_pos % spread
    tp_pos = lax.axis_index("tp")
    local_width = hidden.shape[1]
    gathered = lax.all_gather(hidden, "tp", axis=1, tiled=True)
    model_width = gathered.shape[1]
    rows_dev = gathered.shape[0]
    layer_terms = lax.dynamic_index_in_dim(layer_mod, local_seq, 0, keepdims=False)
    text_count = lax.dynamic_index_in_dim(lengths, local_seq, 0, keepdims=False)
    modulated = modulate(gathered.astype(jnp.float32), layer_terms[0], layer_terms[1]).astype(
        jnp.bfloat16
    )
    head_dim = q_gain.shape[0]
    head_cols = qkv_weight.shape[2]
    heads_here = head_cols // head_dim
    projected = jnp.dot(
        modulated,
        qkv_weight.reshape(model_width, 3 * head_cols),
        preferred_element_type=jnp.float32,
    )
    projected = projected.reshape(rows_dev, 3, heads_here, head_dim)
    cosine, sine_part = rope_angles(positions)
    queries = rotate(rms_gain(projected[:, 0], q_gain), cosine, sine_part).astype(jnp.bfloat16)
    key_rot = rotate(rms_gain(projected[:, 1], k_gain), cosine, sine_part).astype(jnp.bfloat16)
    values = projected[:, 2].astype(jnp.bfloat16)
    packet = jnp.stack([key_rot, values])
    softmax_state = (
        jnp.full((heads_here, rows_dev), -jnp.inf, jnp.float32),
        jnp.zeros((heads_here, rows_dev), jnp.float32),
        jnp.zeros((heads_here, rows_dev, head_dim), jnp.float32),
    )
    held_keys = packet
    for bit_pos in range(bit_count):
        far_keys = swapped(held_keys, "seq", bit_pos)
        block_size = 1 << bit_pos
        lower_half = shard_pos // block_size % 2 == 0
        held_keys = jnp.where(
            lower_half,
            jnp.concatenate([held_keys, far_keys], axis=1),
            jnp.concatenate([far_keys, held_keys], axis=1),
        )
    softmax_state = attend_block(softmax_state, queries, held_keys, 0, text_count)
    row_max, row_sum, weighted = softmax_state
    attended = (weighted / row_sum[:, :, None]).astype(jnp.bfloat16)
    log_sums = row_max + jnp.log(row_sum)
    attn_flat = attended.transpose(1, 0, 2).reshape(rows_dev, head_cols)
    partial_out = jnp.dot(attn_flat, out_weight, preferred_element_type=jnp.float32)
    update = lax.psum_scatter(
        partial_out.astype(jnp.bfloat16), "tp", scatter_dimension=1, tiled=True
    ).astype(jnp.float32)
    gate_slice = lax.dynamic_slice_in_dim(layer_terms[2], tp_pos * local_width, local_width, 0)
    new_hidden = (hidden.astype(jnp.float32) + gate_slice * update).astype(jnp.bfloat16)
    final_terms = lax.dynamic_index_in_dim(final_mod, local_seq, 0, keepdims=False)
    final_shift = lax.dynamic_slice_in_dim(final_terms[0], tp_pos * local_width, local_width, 0)
    final_scale = lax.dynamic_slice_in_dim(final_terms[1], tp_pos * local_width, local_width, 0)
    image_rows = new_hidden[:IMG_DEV].astype(jnp.float32)
    weight = final_weight.astype(jnp.float32)
    row_sums = jnp.sum(image_rows, axis=1)
    squares = jnp.sum(image_rows * image_rows, axis=1)
    row_sums, squares = lax.psum((row_sums, squares), "tp")
    row_mean = row_sums / model_width
    inv_std = lax.rsqrt(squares / model_width - row_mean * row_mean + 1e-06)
    final_in = (image_rows - row_mean[:, None]) * inv_std[:, None] * (
        1.0 + final_scale
    ) + final_shift
    velocity = lax.psum(
        jnp.dot(final_in, weight, precision=lax.Precision.HIGHEST).astype(jnp.bfloat16), "tp"
    ).astype(jnp.float32)
    half_rows = IMG_DEV // 2
    is_cond = local_seq % 2 == 0
    outgoing = jnp.where(is_cond, velocity[half_rows:], velocity[:half_rows])
    partner_half = swapped(outgoing.astype(jnp.bfloat16), "seq", bit_count).astype(outgoing.dtype)
    own_half = jnp.where(is_cond, velocity[:half_rows], velocity[half_rows:])
    cond_vel = jnp.where(is_cond, own_half, partner_half)
    uncond_vel = jnp.where(is_cond, partner_half, own_half)
    guided = uncond_vel + GUIDE * (cond_vel - uncond_vel)
    step_now = step_index[0]
    time_step = sigma_at(step_now + 1) - sigma_at(step_now)
    return (new_hidden, log_sums, latents + time_step * guided)


def solution(mesh):
    return jax.shard_map(
        on_device,
        mesh=mesh,
        in_specs=(
            P(("pair", "seq"), "tp"),
            P(None, ("pair", "seq")),
            P("pair"),
            P(),
            P("pair", None, None),
            P("pair", None, None),
            P(None, None, "tp"),
            P(),
            P(),
            P("tp", None),
            P("tp", None),
            P(("pair", "seq"), None),
        ),
        out_specs=(P(("pair", "seq"), "tp"), P("tp", ("pair", "seq")), P(("pair", "seq"), None)),
        check_vma=False,
    )
```

profile of v0, /device:TPU:2, one launch (start us, length us, event | category | flops | bytes accessed | tf_op | source)
XLA Modules:
  0.0 560.9 jit_solution(13021237416934958148)
XLA Ops:
  8.0 10.3 %copy.17 = bf16[3072,3,384]{0,2,1:T(8,128)(2,1)} copy(bf16[3072,3,384]{2,0,1:T(8,128)(2,1)} %param.20) | data formatting | bytes 14155776 | tf_op args[6]
  20.3 65.6 %all-gather.2.cloned.1.call-done = bf16[576,3072]{1,0:T(8,128)(2,1)} async-done(((bf16[576,768]{1,0:T(8,128)(2,1)}), bf16[576,3072]{1,0:T(8,128)(2,1)}) %all-gather.2.cloned.1.call-update) | async-done | bytes 3538960 | tf_op jit(solution)/shard_map/all_gather | solution.py:119
  85.9 3.3 convert_reduce_fusion
  89.2 8.0 %fusion.26 = f32[576,3,3,128]{3,0,2,1:T(8,128)S(1)} fusion(bf16[3,3,128,3072]{3,2,1,0:T(8,128)(2,1)} %bitcast.68, bf16[576,3072]{1,0:T(8,128)(2,1)S(1)} %copy-done.1, f32[3072]{0:T(1024)S(1)} %bitcast.71, f32[3072]{0:T(1024)S(1)} %bitcast.70, f32[576]{0:T(1024)S(1)} %get-tuple-element.306, f32[576]{0:T(1024)S(1)} %get-tuple-element.305), kind=kOutput, calls=%fused_computation.38 | convolution fusion | flops 4087480320 | bytes 13300224 | tf_op jit(solution)/shard_map/dot_general | solution.py:130
  112.7 3.4 subtract_convert_fusion
  122.5 4.5 collective-permute-start
  127.0 30.3 %collective-permute-done = bf16[2,576,3,128]{3,1,2,0:T(8,128)(2,1)} collective-permute-done((bf16[2,576,3,128]{3,1,2,0:T(8,128)(2,1)}, bf16[2,576,3,128]{3,1,2,0:T(8,128)(2,1)}, u32[]{:S(2)}, u32[]{:S(2)}) %collective-permute-start) | collective-permute-done | bytes 884768 | tf_op jit(solution)/shard_map/ppermute | solution.py:23
  161.0 39.1 %collective-permute-done.1 = bf16[2,1152,3,128]{3,1,2,0:T(8,128)(2,1)} collective-permute-done((bf16[2,1152,3,128]{3,1,2,0:T(8,128)(2,1)}, bf16[2,1152,3,128]{3,1,2,0:T(8,128)(2,1)}, u32[]{:S(2)}, u32[]{:S(2)}) %collective-permute-start.1) | collective-permute-done | bytes 1769504 | tf_op jit(solution)/shard_map/ppermute | solution.py:23
  200.1 5.3 maximum_select_fusion.1
  211.6 71.9 %collective-permute-done.2 = bf16[2,2304,3,128]{3,1,2,0:T(8,128)(2,1)} collective-permute-done((bf16[2,2304,3,128]{3,1,2,0:T(8,128)(2,1)}, bf16[2,2304,3,128]{3,1,2,0:T(8,128)(2,1)}, u32[]{:S(2)}, u32[]{:S(2)}) %collective-permute-start.2) | collective-permute-done | bytes 3538976 | tf_op jit(solution)/shard_map/ppermute | solution.py:23
  283.5 9.3 %maximum_select_fusion = bf16[2,4608,3,128]{3,1,2,0:T(8,128)(2,1)} fusion(bf16[2,2304,3,128]{3,1,2,0:T(8,128)(2,1)} %collective-permute-done.2, bf16[2,2304,3,128]{3,1,2,0:T(8,128)(2,1)} %maximum_select_fusion.1, pred[]{:T(512)S(6)} %eq.18), kind=kLoop, calls=%fused_computation.35 | loop fusion | flops 31850496 | bytes 14155777 | tf_op jit(solution)/shard_map/jit(_where)/select_n | solution.py:151
  292.8 102.5 %while.21 = (s32[]{:T(128)}, f32[3,576]{1,0:T(4,128)S(1)}, f32[3,576]{1,0:T(4,128)S(1)}, f32[3,576,128]{2,1,0:T(8,128)}, s32[]{:T(128)}, /*index=5*/bf16[2,4608,...) while((s32[]{:T(128)}, f32[3,576]{1,0:T(4,128)S(1)}, ...), condition=%wide.region_7.8_spmd.clone.clone, body=%wide.region_4.7_spmd.clone.clone.sunk | while | flops 521231616 | bytes 15596003 | solution.py:95
  293.5 3.9 bitcast_reduce_fusion.2
  300.7 4.7 fusion.72
  306.1 3.9 bitcast_reduce_fusion.2
  313.3 5.0 fusion.72
  318.9 3.9 bitcast_reduce_fusion.2
  326.1 5.0 fusion.72
  331.7 3.9 bitcast_reduce_fusion.2
  339.0 5.0 fusion.72
  344.6 3.9 bitcast_reduce_fusion.2
  351.8 5.0 fusion.72
  357.4 3.9 bitcast_reduce_fusion.2
  364.7 5.0 fusion.72
  370.3 3.9 bitcast_reduce_fusion.2
  377.5 5.0 fusion.72
  383.1 3.9 bitcast_reduce_fusion.2
  390.3 5.0 fusion.72
  397.1 3.8 convolution_convert_fusion
  402.7 80.0 %reduce-scatter.2.cloned.1.call-done = bf16[576,768]{1,0:T(8,128)(2,1)} async-done(((bf16[576,3072]{1,0:T(8,128)(2,1)}), bf16[576,768]{1,0:T(8,128)(2,1)}) %reduce-scatter.2.cloned.1.call-update) | async-done | bytes 884752 | tf_op jit(solution)/shard_map/reduce_scatter | solution.py:162
  485.4 10.7 %all-reduce = (f32[512]{0:T(512)S(1)}, f32[512]{0:T(512)S(1)}) all-reduce(f32[512]{0:T(512)S(1)} %get-tuple-element.267, f32[512]{0:T(512)S(1)} %get-tuple-element.266), channel_id=1, replica_groups=mesh['pair'=2,'seq'=32,'tp'=4] {'tp'}, use_global_device_ids=true, to_apply=%region_12.13 | all-reduce | flops 1024 | bytes 8192 | tf_op jit(solution)/shard_map/psum | solution.py:174
  499.9 48.9 %all-reduce.3.cloned.1.call-done = bf16[512,64]{0,1:T(8,128)(2,1)} async-done(((bf16[512,64]{0,1:T(8,128)(2,1)}), bf16[512,64]{0,1:T(8,128)(2,1)}) %all-reduce.3.cloned.1.call-update) | async-done | bytes 65552 | tf_op jit(solution)/shard_map/psum | solution.py:180
  (117 shorter events, 80.6 us)
Async XLA Ops:
  7.2 389.9 %copy-start = (bf16[384,3072]{1,0:T(8,128)(2,1)S(1)}, bf16[384,3072]{1,0:T(8,128)(2,1)}, u32[]{:S(2)}) copy-start(bf16[384,3072]{1,0:T(8,128)(2,1)} %param.23) | copy-start | bytes 7077892
  7.2 78.7 %all-gather.2.cloned.1.call-start = ((), (), s32[]{:S(2)}) async-start(), calls=%async_computation.1 | async-start | bytes 4423680 | tf_op jit(solution)/shard_map/all_gather | solution.py:119
  7.9 474.8 %reduce-scatter.2.cloned.1.call-start = ((), (), s32[]{:S(2)}) async-start(), calls=%async_computation.2 | async-start | bytes 4423680 | tf_op jit(solution)/shard_map/reduce_scatter | solution.py:162
  8.0 10.3 %copy-start.8 = (f32[128]{0:T(128)S(1)}, f32[128]{0:T(128)}, u32[]{:S(2)}) copy-start(f32[128]{0:T(128)} %param.22) | copy-start | bytes 1540
  8.0 10.4 %copy-start.9 = (f32[128]{0:T(128)S(1)}, f32[128]{0:T(128)}, u32[]{:S(2)}) copy-start(f32[128]{0:T(128)} %param.21) | copy-start | bytes 1540
  8.0 10.6 %copy-start.7 = (s32[3,576]{1,0:T(4,128)S(1)}, s32[3,576]{1,0:T(4,128)}, u32[]{:S(2)}) copy-start(s32[3,576]{1,0:T(4,128)} %param.15) | copy-start | bytes 20740
  85.9 3.3 copy-start.1
  122.5 34.9 %collective-permute-start = (bf16[2,576,3,128]{3,1,2,0:T(8,128)(2,1)}, bf16[2,576,3,128]{3,1,2,0:T(8,128)(2,1)}, u32[]{:S(2)}, u32[]{:S(2)}) collective-permute-start(bf16[2,576,3,128]{3,1,2,0:T(8,128)(2,1)} %pad_maximum_fusion), channel_id=1, source_target_pairs={{0,4},{4,0},{8,12},{12,8},{16,20},{20,16},{24,28},{28,24},{32,36},... | collective-permute-start | bytes 2654216 | tf_op jit(solution)/shard_map/ppermute | solution.py:23
  160.4 39.7 %collective-permute-start.1 = (bf16[2,1152,3,128]{3,1,2,0:T(8,128)(2,1)}, bf16[2,1152,3,128]{3,1,2,0:T(8,128)(2,1)}, u32[]{:S(2)}, u32[]{:S(2)}) collective-permute-start(bf16[2,1152,3,128]{3,1,2,0:T(8,128)(2,1)} %maximum_select_fusion.2), channel_id=1, source_target_pairs={{0,8},{8,0},{4,12},{12,4},{16,24},{24,16},{20,28},{28,20},{32,40},... | collective-permute-start | bytes 5308424 | tf_op jit(solution)/shard_map/ppermute | solution.py:23
  161.0 46.4 %copy-start.11 = (s32[4]{0:T(128)S(1)}, s32[4]{0:T(128)}, u32[]{:S(2)}) copy-start(s32[4]{0:T(128)} %param.16) | copy-start | bytes 52
  161.0 47.0 %copy-start.4 = (bf16[576,3,64,1]{0,3,2,1:T(2,128)(2,1)S(1)}, bf16[576,3,64,1]{0,3,2,1:T(2,128)(2,1)}, u32[]{:S(2)}) copy-start(bf16[576,3,64,1]{0,3,2,1:T(2,128)(2,1)} %get-tuple-element.295) | copy-start | bytes 663556
  161.0 47.0 %copy-start.5 = (bf16[576,3,64,1]{0,3,2,1:T(2,128)(2,1)S(1)}, bf16[576,3,64,1]{0,3,2,1:T(2,128)(2,1)}, u32[]{:S(2)}) copy-start(bf16[576,3,64,1]{0,3,2,1:T(2,128)(2,1)} %get-tuple-element.296) | copy-start | bytes 663556
  205.4 78.2 %collective-permute-start.2 = (bf16[2,2304,3,128]{3,1,2,0:T(8,128)(2,1)}, bf16[2,2304,3,128]{3,1,2,0:T(8,128)(2,1)}, u32[]{:S(2)}, u32[]{:S(2)}) collective-permute-start(bf16[2,2304,3,128]{3,1,2,0:T(8,128)(2,1)} %maximum_select_fusion.1), channel_id=1, source_target_pairs={{0,16},{16,0},{4,20},{20,4},{8,24},{24,8},{12,28},{28,12},{32,48},... | collective-permute-start | bytes 10616840 | tf_op jit(solution)/shard_map/ppermute | solution.py:23
  400.8 81.8 %copy-start.2 = (bf16[576,768]{1,0:T(8,128)(2,1)S(1)}, bf16[576,768]{1,0:T(8,128)(2,1)}, u32[]{:S(2)}) copy-start(bf16[576,768]{1,0:T(8,128)(2,1)} %param.14) | copy-start | bytes 2654212
  400.8 95.3 %copy-start.10 = (bf16[768,64]{0,1:T(8,128)(2,1)S(1)}, bf16[768,64]{0,1:T(8,128)(2,1)}, u32[]{:S(2)}) copy-start(bf16[768,64]{0,1:T(8,128)(2,1)} %param.24) | copy-start | bytes 294916
  400.9 152.8 %copy-start.6 = (f32[256,64]{0,1:T(8,128)S(1)}, f32[256,64]{0,1:T(8,128)}, u32[]{:S(2)}) copy-start(f32[256,64]{0,1:T(8,128)} %param.25) | copy-start | bytes 196612
  400.9 147.9 %all-reduce.3.cloned.1.call-start = ((), (), s32[]{:S(2)}) async-start(), calls=%async_computation.3 | async-start | bytes 131072 | tf_op jit(solution)/shard_map/psum | solution.py:180
  484.1 0.9 copy-start.3
  549.7 4.0 collective-permute-start.3
Sparse Core Ops, SparseCore 0:
  9.8 76.0 all-gather.1
  401.0 81.6 reduce-scatter.1
  499.3 49.4 all-reduce.2
where the time goes:
time: 563 us; the launch traced here: 561 us
  waiting for transfers between devices  338 us (60%)
  matrix products  85.7 us (15%)
  other arithmetic  73.4 us (13%)
  local copies, waits for them, and re-layouts  28.9 us (5%)
  between operations  14.7 us (3%)
  blocking collectives  10.7 us (2%)
  starting transfers between devices  8.84 us (2%)
    ppermute x4, waiting for transfers between devices, swapped(): return lax.ppermute(block, axis, route)  143 us
    reduce_scatter x1, waiting for transfers between devices, on_device(): lax.psum_scatter(partial_out.astype(jnp.bfloat16), 'tp', scatter_dimensio...  80 us
    all_gather x1, waiting for transfers between devices, on_device(): gathered = lax.all_gather(hidden, 'tp', axis=1, tiled=True)  65.6 us
    psum x1, waiting for transfers between devices, on_device(): lax.psum(jnp.dot(final_in, weight, precision=lax.Precision.HIGHEST).astyp...  48.9 us
    dot_general x8, matrix products, fold_piece(): jnp.einsum('hqk,khd->hqd', exps.astype(jnp.bfloat16), key_piece[1], prefe...  39.4 us
    dot_general x8, matrix products, fold_piece(): jnp.einsum('qhd,khd->hqk', queries, key_piece[0], preferred_element_type=...  31.6 us
    reduce_sum x8, other arithmetic, fold_piece(): row_sum = row_sum * decay + jnp.sum(exps, axis=2)  25.9 us
    select_n x3, other arithmetic, on_device(): jnp.where(lower_half, jnp.concatenate([held_keys, far_keys], axis=1), jnp...  17.7 us
  transfers between devices with their start and end apart: 7, of which 7 were waited for; matrix products, arithmetic and copies ran while one was open for 3% of the time, Pallas kernels for 0%

commit v1 on v0

--- a/solution.py
+++ b/solution.py
@@ -177,8 +177,11 @@
     final_in = (image_rows - row_mean[:, None]) * inv_std[:, None] * (
         1.0 + final_scale
     ) + final_shift
-    velocity = lax.psum(
-        jnp.dot(final_in, weight, precision=lax.Precision.HIGHEST).astype(jnp.bfloat16), "tp"
+    velocity = jnp.sum(
+        lax.all_gather(
+            jnp.dot(final_in, weight, precision=lax.Precision.HIGHEST).astype(jnp.bfloat16), "tp"
+        ),
+        axis=0,
     ).astype(jnp.float32)
     half_rows = IMG_DEV // 2
     is_cond = local_seq % 2 == 0

time: 563 us -> 526 us (0.934)
  waiting for transfers between devices: 338 us -> 289 us
  blocking collectives: 10.7 us -> 24.6 us
    psum x1 -> x0, waiting for transfers between devices: 48.9 us -> none  [on_device(): lax.psum(jnp.dot(final_in, weight, precision=lax.Precision.HIGHEST).astyp...]
    all_gather x0 -> x1, blocking collectives: none -> 13.9 us  [on_device(): lax.all_gather(jnp.dot(final_in, weight, precision=lax.Precision.HIGHEST)...]
  transfers between devices with their start and end apart: 7 -> 6, of which waited for: 7 -> 6; matrix products, arithmetic and copies ran while one was open for 3% -> 4% of each run, Pallas kernels for 0% -> 0%
where the time goes in v1:
time: 526 us; the launch traced here: 524 us
  waiting for transfers between devices  289 us (55%)
  matrix products  85.1 us (16%)
  other arithmetic  72.9 us (14%)
  local copies, waits for them, and re-layouts  29 us (6%)
  blocking collectives  24.6 us (5%)
  between operations  15.1 us (3%)
  starting transfers between devices  8.8 us (2%)
    ppermute x4, waiting for transfers between devices, swapped(): return lax.ppermute(block, axis, route)  143 us
    reduce_scatter x1, waiting for transfers between devices, on_device(): lax.psum_scatter(partial_out.astype(jnp.bfloat16), 'tp', scatter_dimensio...  79.3 us
    all_gather x1, waiting for transfers between devices, on_device(): gathered = lax.all_gather(hidden, 'tp', axis=1, tiled=True)  65.6 us
    dot_general x8, matrix products, fold_piece(): jnp.einsum('hqk,khd->hqd', exps.astype(jnp.bfloat16), key_piece[1], prefe...  39.4 us
    dot_general x8, matrix products, fold_piece(): jnp.einsum('qhd,khd->hqk', queries, key_piece[0], preferred_element_type=...  31.6 us
    reduce_sum x8, other arithmetic, fold_piece(): row_sum = row_sum * decay + jnp.sum(exps, axis=2)  25.9 us
    select_n x3, other arithmetic, on_device(): jnp.where(lower_half, jnp.concatenate([held_keys, far_keys], axis=1), jnp...  17.7 us
    all_gather x1, blocking collectives, on_device(): lax.all_gather(jnp.dot(final_in, weight, precision=lax.Precision.HIGHEST)...  13.9 us
  transfers between devices with their start and end apart: 6, of which 6 were waited for; matrix products, arithmetic and copies ran while one was open for 4% of the time, Pallas kernels for 0%

profile of v1, /device:TPU:2, one launch (start us, length us, event | category | flops | bytes accessed | tf_op | source)
XLA Modules:
  0.0 524.4 jit_solution(2363377369706950411)
XLA Ops:
  8.0 10.3 %copy.17 = bf16[3072,3,384]{0,2,1:T(8,128)(2,1)} copy(bf16[3072,3,384]{2,0,1:T(8,128)(2,1)} %param.20) | data formatting | bytes 14155776 | tf_op args[6]
  20.3 65.6 %all-gather.3.cloned.1.call-done = bf16[576,3072]{1,0:T(8,128)(2,1)} async-done(((bf16[576,768]{1,0:T(8,128)(2,1)}), bf16[576,3072]{1,0:T(8,128)(2,1)}) %all-gather.3.cloned.1.call-update) | async-done | bytes 3538960 | tf_op jit(solution)/shard_map/all_gather | solution.py:119
  85.9 3.3 convert_reduce_fusion
  89.2 8.0 %fusion.26 = f32[576,3,3,128]{3,0,2,1:T(8,128)S(1)} fusion(bf16[3,3,128,3072]{3,2,1,0:T(8,128)(2,1)} %bitcast.70, bf16[576,3072]{1,0:T(8,128)(2,1)S(1)} %copy-done.1, f32[3072]{0:T(1024)S(1)} %bitcast.73, f32[3072]{0:T(1024)S(1)} %bitcast.72, f32[576]{0:T(1024)S(1)} %get-tuple-element.306, f32[576]{0:T(1024)S(1)} %get-tuple-element.305), kind=kOutput, calls=%fused_computation.38 | convolution fusion | flops 4087480320 | bytes 13300224 | tf_op jit(solution)/shard_map/dot_general | solution.py:130
  112.7 3.4 subtract_convert_fusion
  122.5 4.5 collective-permute-start
  127.0 30.3 %collective-permute-done = bf16[2,576,3,128]{3,1,2,0:T(8,128)(2,1)} collective-permute-done((bf16[2,576,3,128]{3,1,2,0:T(8,128)(2,1)}, bf16[2,576,3,128]{3,1,2,0:T(8,128)(2,1)}, u32[]{:S(2)}, u32[]{:S(2)}) %collective-permute-start) | collective-permute-done | bytes 884768 | tf_op jit(solution)/shard_map/ppermute | solution.py:23
  161.0 39.1 %collective-permute-done.1 = bf16[2,1152,3,128]{3,1,2,0:T(8,128)(2,1)} collective-permute-done((bf16[2,1152,3,128]{3,1,2,0:T(8,128)(2,1)}, bf16[2,1152,3,128]{3,1,2,0:T(8,128)(2,1)}, u32[]{:S(2)}, u32[]{:S(2)}) %collective-permute-start.1) | collective-permute-done | bytes 1769504 | tf_op jit(solution)/shard_map/ppermute | solution.py:23
  200.1 5.3 %maximum_select_fusion.1 = bf16[2,2304,3,128]{3,1,2,0:T(8,128)(2,1)} fusion(bf16[2,1152,3,128]{3,1,2,0:T(8,128)(2,1)} %collective-permute-done.1, bf16[2,1152,3,128]{3,1,2,0:T(8,128)(2,1)} %maximum_select_fusion.2, pred[]{:T(512)S(6)} %eq.19), kind=kLoop, calls=%fused_computation.39 | loop fusion | flops 15925248 | bytes 7077889 | tf_op jit(solution)/shard_map/jit(_where)/select_n | solution.py:151
  211.6 71.9 %collective-permute-done.2 = bf16[2,2304,3,128]{3,1,2,0:T(8,128)(2,1)} collective-permute-done((bf16[2,2304,3,128]{3,1,2,0:T(8,128)(2,1)}, bf16[2,2304,3,128]{3,1,2,0:T(8,128)(2,1)}, u32[]{:S(2)}, u32[]{:S(2)}) %collective-permute-start.2) | collective-permute-done | bytes 3538976 | tf_op jit(solution)/shard_map/ppermute | solution.py:23
  283.5 9.3 %maximum_select_fusion = bf16[2,4608,3,128]{3,1,2,0:T(8,128)(2,1)} fusion(bf16[2,2304,3,128]{3,1,2,0:T(8,128)(2,1)} %collective-permute-done.2, bf16[2,2304,3,128]{3,1,2,0:T(8,128)(2,1)} %maximum_select_fusion.1, pred[]{:T(512)S(6)} %eq.18), kind=kLoop, calls=%fused_computation.35 | loop fusion | flops 31850496 | bytes 14155777 | tf_op jit(solution)/shard_map/jit(_where)/select_n | solution.py:151
  292.8 102.5 %while.21 = (s32[]{:T(128)}, f32[3,576]{1,0:T(4,128)S(1)}, f32[3,576]{1,0:T(4,128)S(1)}, f32[3,576,128]{2,1,0:T(8,128)}, s32[]{:T(128)}, /*index=5*/bf16[2,4608,...) while((s32[]{:T(128)}, f32[3,576]{1,0:T(4,128)S(1)}, ...), condition=%wide.region_7.8_spmd.clone.clone, body=%wide.region_4.7_spmd.clone.clone.sunk | while | flops 521231616 | bytes 15596003 | solution.py:95
  293.5 3.9 bitcast_reduce_fusion.2
  300.7 4.7 fusion.72
  306.1 3.9 bitcast_reduce_fusion.2
  313.3 5.0 fusion.72
  318.9 3.9 bitcast_reduce_fusion.2
  326.1 5.0 fusion.72
  331.7 3.9 bitcast_reduce_fusion.2
  339.0 5.0 fusion.72
  344.6 3.9 bitcast_reduce_fusion.2
  351.8 5.0 fusion.72
  357.4 3.9 bitcast_reduce_fusion.2
  364.7 5.0 fusion.72
  370.3 3.9 bitcast_reduce_fusion.2
  377.5 5.0 fusion.72
  383.1 3.9 bitcast_reduce_fusion.2
  390.3 5.0 fusion.72
  397.1 3.8 convolution_convert_fusion
  403.4 79.3 %reduce-scatter.2.cloned.1.call-done = bf16[576,768]{1,0:T(8,128)(2,1)} async-done(((bf16[576,3072]{1,0:T(8,128)(2,1)}), bf16[576,768]{1,0:T(8,128)(2,1)}) %reduce-scatter.2.cloned.1.call-update) | async-done | bytes 884752 | tf_op jit(solution)/shard_map/reduce_scatter | solution.py:162
  485.4 10.7 %all-reduce = (f32[512]{0:T(512)S(1)}, f32[512]{0:T(512)S(1)}) all-reduce(f32[512]{0:T(512)S(1)} %get-tuple-element.267, f32[512]{0:T(512)S(1)} %get-tuple-element.266), channel_id=1, replica_groups=mesh['pair'=2,'seq'=32,'tp'=4] {'tp'}, use_global_device_ids=true, to_apply=%region_12.13 | all-reduce | flops 1024 | bytes 8192 | tf_op jit(solution)/shard_map/psum | solution.py:174
  498.5 13.9 %all-gather = bf16[2048,64]{0,1:T(8,128)(2,1)S(1)} all-gather(bf16[512,64]{0,1:T(8,128)(2,1)S(1)} %fusion.38), channel_id=2, replica_groups=mesh['pair'=2,'seq'=32,'tp'=4] {'tp'}, dimensions={0}, use_global_device_ids=true | all-gather | bytes 327680 | tf_op jit(solution)/shard_map/all_gather | solution.py:181
  (117 shorter events, 79.5 us)
Async XLA Ops:
  7.2 389.9 %copy-start = (bf16[384,3072]{1,0:T(8,128)(2,1)S(1)}, bf16[384,3072]{1,0:T(8,128)(2,1)}, u32[]{:S(2)}) copy-start(bf16[384,3072]{1,0:T(8,128)(2,1)} %param.23) | copy-start | bytes 7077892
  7.2 78.7 %all-gather.3.cloned.1.call-start = ((), (), s32[]{:S(2)}) async-start(), calls=%async_computation.1 | async-start | bytes 4423680 | tf_op jit(solution)/shard_map/all_gather | solution.py:119
  7.9 474.8 %reduce-scatter.2.cloned.1.call-start = ((), (), s32[]{:S(2)}) async-start(), calls=%async_computation.2 | async-start | bytes 4423680 | tf_op jit(solution)/shard_map/reduce_scatter | solution.py:162
  8.0 10.3 %copy-start.8 = (f32[128]{0:T(128)S(1)}, f32[128]{0:T(128)}, u32[]{:S(2)}) copy-start(f32[128]{0:T(128)} %param.22) | copy-start | bytes 1540
  8.0 10.4 %copy-start.9 = (f32[128]{0:T(128)S(1)}, f32[128]{0:T(128)}, u32[]{:S(2)}) copy-start(f32[128]{0:T(128)} %param.21) | copy-start | bytes 1540
  8.0 10.6 %copy-start.7 = (s32[3,576]{1,0:T(4,128)S(1)}, s32[3,576]{1,0:T(4,128)}, u32[]{:S(2)}) copy-start(s32[3,576]{1,0:T(4,128)} %param.15) | copy-start | bytes 20740
  85.9 3.3 copy-start.1
  122.5 34.9 %collective-permute-start = (bf16[2,576,3,128]{3,1,2,0:T(8,128)(2,1)}, bf16[2,576,3,128]{3,1,2,0:T(8,128)(2,1)}, u32[]{:S(2)}, u32[]{:S(2)}) collective-permute-start(bf16[2,576,3,128]{3,1,2,0:T(8,128)(2,1)} %pad_maximum_fusion), channel_id=1, source_target_pairs={{0,4},{4,0},{8,12},{12,8},{16,20},{20,16},{24,28},{28,24},{32,36},... | collective-permute-start | bytes 2654216 | tf_op jit(solution)/shard_map/ppermute | solution.py:23
  160.4 39.7 %collective-permute-start.1 = (bf16[2,1152,3,128]{3,1,2,0:T(8,128)(2,1)}, bf16[2,1152,3,128]{3,1,2,0:T(8,128)(2,1)}, u32[]{:S(2)}, u32[]{:S(2)}) collective-permute-start(bf16[2,1152,3,128]{3,1,2,0:T(8,128)(2,1)} %maximum_select_fusion.2), channel_id=1, source_target_pairs={{0,8},{8,0},{4,12},{12,4},{16,24},{24,16},{20,28},{28,20},{32,40},... | collective-permute-start | bytes 5308424 | tf_op jit(solution)/shard_map/ppermute | solution.py:23
  161.0 46.4 %copy-start.11 = (s32[4]{0:T(128)S(1)}, s32[4]{0:T(128)}, u32[]{:S(2)}) copy-start(s32[4]{0:T(128)} %param.16) | copy-start | bytes 52
  161.0 47.0 %copy-start.4 = (bf16[576,3,64,1]{0,3,2,1:T(2,128)(2,1)S(1)}, bf16[576,3,64,1]{0,3,2,1:T(2,128)(2,1)}, u32[]{:S(2)}) copy-start(bf16[576,3,64,1]{0,3,2,1:T(2,128)(2,1)} %get-tuple-element.295) | copy-start | bytes 663556
  161.0 47.0 %copy-start.5 = (bf16[576,3,64,1]{0,3,2,1:T(2,128)(2,1)S(1)}, bf16[576,3,64,1]{0,3,2,1:T(2,128)(2,1)}, u32[]{:S(2)}) copy-start(bf16[576,3,64,1]{0,3,2,1:T(2,128)(2,1)} %get-tuple-element.296) | copy-start | bytes 663556
  205.4 78.2 %collective-permute-start.2 = (bf16[2,2304,3,128]{3,1,2,0:T(8,128)(2,1)}, bf16[2,2304,3,128]{3,1,2,0:T(8,128)(2,1)}, u32[]{:S(2)}, u32[]{:S(2)}) collective-permute-start(bf16[2,2304,3,128]{3,1,2,0:T(8,128)(2,1)} %maximum_select_fusion.1), channel_id=1, source_target_pairs={{0,16},{16,0},{4,20},{20,4},{8,24},{24,8},{12,28},{28,12},{32,48},... | collective-permute-start | bytes 10616840 | tf_op jit(solution)/shard_map/ppermute | solution.py:23
  400.8 81.8 %copy-start.2 = (bf16[576,768]{1,0:T(8,128)(2,1)S(1)}, bf16[576,768]{1,0:T(8,128)(2,1)}, u32[]{:S(2)}) copy-start(bf16[576,768]{1,0:T(8,128)(2,1)} %param.14) | copy-start | bytes 2654212
  400.8 95.3 %copy-start.10 = (bf16[768,64]{0,1:T(8,128)(2,1)S(1)}, bf16[768,64]{0,1:T(8,128)(2,1)}, u32[]{:S(2)}) copy-start(bf16[768,64]{0,1:T(8,128)(2,1)} %param.24) | copy-start | bytes 294916
  403.4 113.5 %copy-start.6 = (f32[256,64]{0,1:T(8,128)S(1)}, f32[256,64]{0,1:T(8,128)}, u32[]{:S(2)}) copy-start(f32[256,64]{0,1:T(8,128)} %param.25) | copy-start | bytes 196612
  484.1 0.9 copy-start.3
  512.9 4.0 collective-permute-start.3
Sparse Core Ops, SparseCore 0:
  9.8 76.0 all-gather.2
  401.0 81.6 reduce-scatter.1
